TPU v7x, 128 devices: a whole 4x4x4 slice. The times are simulated.
128 devices in a mesh: seq: 32 (over y, z, core), head: 4 (over x).
Axes of the slice: x: 4, y: 4, z: 4, core: 2. Of those that a mesh axis runs over, the one named last changes fastest.
Arguments:
- queries: bfloat16 [8192, 2048], P('seq', 'head'), parts along dimension 1, may hold values from -6 to 6
- keys: bfloat16 [8192, 512], P('seq', 'head'), parts along dimension 1, may hold values from -6 to 6
- values: bfloat16 [8192, 512], P('seq', 'head'), parts along dimension 1, may hold values from -6 to 6
- grad_out: bfloat16 [8192, 2048], P('seq', 'head'), parts along dimension 1, may hold values from -6 to 6
- lengths: int32 [16], replicated, may hold values from 1 to 2048, 8192 in all
- send_order: int32 [32, 256], replicated, may hold values from 0 to 255, each once within a row
Outputs:
- attended: float32 [8192, 2048], P('seq', 'head'), parts along dimension 1
- grad_queries: float32 [8192, 2048], P('seq', 'head'), parts along dimension 1
- grad_keys: float32 [8192, 512], P('seq', 'head'), parts along dimension 1
- grad_values: float32 [8192, 512], P('seq', 'head'), parts along dimension 1
There are 4 independent parts, one for each index of `head`. A program takes and returns all parts, laid end to end along the dimension named above; an argument that names none is the same for every part. Nothing has to cross between parts.
Inputs may be any that keep to these rules, and one draw needn't show every extreme that they name: `lengths`: they sum to 8192; the longest is exactly 2048. `send_order`: each row is a permutation of 0 to 255.
All inputs are finite; a program needn't handle non-finite values.
Results may differ from a plain program's by a relative error of at most 0.039.
Values may be sent and summed in bfloat16 or wider, within the bound.
No kernel may reach another device: no remote copies, remote signals or barrier semaphores. Data moves between devices by JAX's collectives and lax.ppermute only.
A program may use at most 64 MiB of HBM per device.

v0:
```python
import math
import jax
import jax.numpy as jnp
from jax import lax
from jax.sharding import PartitionSpec as P

masked_value = -1e30


def doc_index(positions, bounds):
    return jnp.sum((positions[:, None] >= bounds[None, :]).astype(jnp.int32), axis=1)


def visible(query_pos, query_doc, key_pos, bounds):
    key_doc = doc_index(key_pos, bounds)
    return ((query_doc[:, None] == key_doc[None, :]) & (key_pos[None, :] <= query_pos[:, None]))[
        :, None, :
    ]


def block_scores(query_heads, key_block, allowed, score_scale):
    products = (
        jnp.einsum("bhd,td->bht", query_heads, key_block, preferred_element_type=jnp.float32)
        * score_scale
    )
    return jnp.where(allowed, products, masked_value)


def key_blocks(key_piece, value_piece):
    piece_rows = key_piece.shape[0]
    block_rows = math.gcd(piece_rows, 512)
    block_count = piece_rows // block_rows
    offsets = block_rows * jnp.arange(block_count, dtype=jnp.int32)
    stacked = (
        key_piece.reshape(block_count, block_rows, key_piece.shape[1]),
        value_piece.reshape(block_count, block_rows, value_piece.shape[1]),
        offsets,
    )
    return (stacked, block_rows)


def forward_piece(run_state, key_piece, value_piece, context):
    query_heads, query_pos, query_doc, bounds, score_scale = context
    stacked, block_rows = key_blocks(key_piece, value_piece)

    def forward_update(loop_state, block_item):
        run_max, run_total, weighted = loop_state
        key_block, value_block, offset = block_item
        allowed = visible(
            query_pos, query_doc, offset + jnp.arange(block_rows, dtype=jnp.int32), bounds
        )
        scores = block_scores(query_heads, key_block, allowed, score_scale)
        new_max = jnp.maximum(run_max, jnp.max(scores, axis=2))
        exp_weights = jnp.where(allowed, jnp.exp(scores - new_max[:, :, None]), 0.0)
        rescale = jnp.exp(run_max - new_max)
        run_total = run_total * rescale + jnp.sum(exp_weights, axis=2)
        weighted = weighted * rescale[:, :, None] + jnp.einsum(
            "bht,td->bhd",
            exp_weights.astype(jnp.bfloat16),
            value_block,
            preferred_element_type=jnp.float32,
        )
        return ((new_max, run_total, weighted), None)

    run_state, _ = lax.scan(forward_update, run_state, stacked)
    return run_state


def backward_piece(key_piece, value_piece, context):
    query_heads, grad_heads, query_pos, query_doc, bounds, score_scale, log_total, out_dot = context
    stacked, block_rows = key_blocks(key_piece, value_piece)

    def backward_update(query_sum, block_item):
        key_block, value_block, offset = block_item
        allowed = visible(
            query_pos, query_doc, offset + jnp.arange(block_rows, dtype=jnp.int32), bounds
        )
        scores = block_scores(query_heads, key_block, allowed, score_scale)
        weights = jnp.where(allowed, jnp.exp(scores - log_total[:, :, None]), 0.0)
        grad_dots = jnp.einsum(
            "bhd,td->bht", grad_heads, value_block, preferred_element_type=jnp.float32
        )
        score_grads = (weights * (grad_dots - out_dot[:, :, None])).astype(jnp.bfloat16)
        query_sum = query_sum + jnp.einsum(
            "bht,td->bhd", score_grads, key_block, preferred_element_type=jnp.float32
        )
        key_term = (
            jnp.einsum("bht,bhd->td", score_grads, query_heads, preferred_element_type=jnp.float32)
            * score_scale
        )
        value_term = jnp.einsum(
            "bht,bhd->td",
            weights.astype(jnp.bfloat16),
            grad_heads,
            preferred_element_type=jnp.float32,
        )
        return (query_sum, (key_term, value_term))

    zero_query = jnp.zeros(query_heads.shape, jnp.float32)
    query_add, (key_terms, value_terms) = lax.scan(backward_update, zero_query, stacked)
    piece_rows = key_piece.shape[0]
    return (query_add, key_terms.reshape(piece_rows, -1), value_terms.reshape(piece_rows, -1))


def per_device(queries, keys, values, grad_out, lengths, send_order):
    shard_count = lax.axis_size("seq")
    my_index = lax.axis_index("seq")
    tok_rows, head_dim = keys.shape
    group_rows = tok_rows // shard_count
    head_count = queries.shape[1] // head_dim
    score_scale = 1.0 / math.sqrt(head_dim)
    bounds = jnp.cumsum(lengths)
    own_order = lax.dynamic_index_in_dim(send_order, my_index, 0, keepdims=False)
    outgoing = jnp.take(queries, own_order, axis=0)
    picked = lax.all_to_all(outgoing, "seq", split_axis=0, concat_axis=0, tiled=True)
    columns = lax.dynamic_slice_in_dim(send_order, my_index * group_rows, group_rows, 1)
    query_pos = (jnp.arange(shard_count, dtype=jnp.int32)[:, None] * tok_rows + columns).reshape(
        tok_rows
    )
    query_doc = doc_index(query_pos, bounds)
    query_heads = picked.reshape(tok_rows, head_count, head_dim)
    grad_heads = grad_out.reshape(tok_rows, head_count, head_dim)
    context = (query_heads, query_pos, query_doc, bounds, score_scale)
    start_state = (
        jnp.full((tok_rows, head_count), masked_value, jnp.float32),
        jnp.zeros((tok_rows, head_count), jnp.float32),
        jnp.zeros((tok_rows, head_count, head_dim), jnp.float32),
    )
    piece_pair = (
        lax.all_gather(keys, "seq", axis=0, tiled=True),
        lax.all_gather(values, "seq", axis=0, tiled=True),
    )
    run_max, run_total, weighted = forward_piece(start_state, piece_pair[0], piece_pair[1], context)
    attended = weighted / run_total[:, :, None]
    attended_low = attended.astype(jnp.bfloat16)
    log_total = run_max + jnp.log(run_total)
    out_dot = jnp.sum(grad_heads.astype(jnp.float32) * attended_low.astype(jnp.float32), axis=2)
    grad_context = (
        query_heads,
        grad_heads,
        query_pos,
        query_doc,
        bounds,
        score_scale,
        log_total,
        out_dot,
    )
    piece_pair = (
        lax.all_gather(keys, "seq", axis=0, tiled=True),
        lax.all_gather(values, "seq", axis=0, tiled=True),
    )
    query_add, key_part, value_part = backward_piece(piece_pair[0], piece_pair[1], grad_context)
    key_all = key_part
    value_all = value_part
    query_sum, key_all, value_all = (query_add, key_all, value_all)
    key_grad, value_grad = (
        lax.psum_scatter(key_all, "seq", scatter_dimension=0, tiled=True),
        lax.psum_scatter(value_all, "seq", scatter_dimension=0, tiled=True),
    )
    grad_queries = (query_sum * score_scale).reshape(tok_rows, head_count * head_dim)
    return (attended.reshape(tok_rows, head_count * head_dim), grad_queries, key_grad, value_grad)


def solution(mesh):
    placed = (P("seq", "head"), P("seq", "head"), P("seq", "head"), P("seq", "head"), P(), P())
    return jax.shard_map(
        per_device,
        mesh=mesh,
        in_specs=placed,
        out_specs=(P("seq", "head"), P("seq", "head"), P("seq", "head"), P("seq", "head")),
        check_vma=False,
    )
```

profile of v0, /device:TPU:0, one launch (start us, length us, event | category | flops | bytes accessed | tf_op | source)
XLA Modules:
  0.0 495.6 jit_solution(17738057707198617605)
XLA Ops:
  12.2 8.4 %all-to-all-start = ((bf16[32,8,512]{2,1,0:T(8,128)(2,1)}), bf16[32,8,512]{2,1,0:T(8,128)(2,1)S(1)}, u32[]{:S(2)}, u32[]{:S(2)}) async-start(bf16[32,8,512]{2,1,0:T(8,128)(2,1)} %bitcast_select_fusion.2), calls=%async_computation | async-start | bytes 524288 | tf_op jit(solution)/shard_map/all_to_all | solution.py:115
  21.8 8.0 %all-to-all-done = bf16[32,8,512]{2,1,0:T(8,128)(2,1)S(1)} async-done(((bf16[32,8,512]{2,1,0:T(8,128)(2,1)}), bf16[32,8,512]{2,1,0:T(8,128)(2,1)S(1)}, u32[]{:S(2)}, u32[]{:S(2)}) %all-to-all-start) | async-done | bytes 262176 | tf_op jit(solution)/shard_map/all_to_all | solution.py:115
  29.9 26.8 %all-gather.3.cloned.1.call-done = bf16[8192,128]{1,0:T(8,128)(2,1)} async-done(((bf16[256,128]{1,0:T(8,128)(2,1)}), bf16[8192,128]{1,0:T(8,128)(2,1)}) %all-gather.3.cloned.1.call-update) | async-done | bytes 2097168 | tf_op jit(solution)/shard_map/all_gather | solution.py:130
  56.7 45.3 %all-gather.5.cloned.1.call-done = bf16[8192,128]{1,0:T(8,128)(2,1)} async-done(((bf16[256,128]{1,0:T(8,128)(2,1)}), bf16[8192,128]{1,0:T(8,128)(2,1)}) %all-gather.5.cloned.1.call-update) | async-done | bytes 2097168 | tf_op jit(solution)/shard_map/all_gather | solution.py:131
  102.0 85.3 %while.32 = (s32[]{:T(128)}, f32[256,4]{0,1:T(4,128)S(1)}, f32[256,4]{0,1:T(4,128)S(1)}, f32[256,4,128]{2,0,1:T(8,128)S(1)}, s32[256]{0:T(256)S(1)}, /*index=5*/...) while((s32[]{:T(128)}, f32[256,4]{0,1:T(4,128)S(1)}, ...), condition=%wide.wide.region_6.7_spmd.clone, body=%wide.wide.region_2.6_spmd.clone.sunk | while | flops 276067328 | bytes 8466673 | solution.py:65
  105.5 1.8 convolution_add_fusion.6
  108.9 1.4 fusion.88
  110.8 1.8 convolution_add_fusion.6
  114.2 1.4 fusion.88
  116.2 1.8 convolution_add_fusion.6
  121.5 1.8 convolution_add_fusion.6
  124.9 1.4 fusion.88
  126.8 1.8 convolution_add_fusion.6
  130.2 1.4 fusion.88
  132.1 1.8 convolution_add_fusion.6
  137.5 1.8 convolution_add_fusion.6
  140.8 1.4 fusion.88
  142.8 1.8 convolution_add_fusion.6
  146.2 1.4 fusion.88
  148.1 1.8 convolution_add_fusion.6
  153.5 1.8 convolution_add_fusion.6
  156.8 1.4 fusion.88
  158.8 1.8 convolution_add_fusion.6
  162.2 1.4 fusion.88
  164.1 1.8 convolution_add_fusion.6
  169.5 1.8 convolution_add_fusion.6
  174.8 1.8 convolution_add_fusion.6
  180.1 1.8 convolution_add_fusion.6
  185.5 1.8 convolution_add_fusion.6
  187.6 133.8 %while.33 = (s32[]{:T(128)}, f32[256,4,128]{2,0,1:T(8,128)S(1)}, f32[16,512,128]{2,1,0:T(8,128)}, f32[16,512,128]{2,1,0:T(8,128)}, s32[256]{0:T(256)S(1)}, /*ind...) while((s32[]{:T(128)}, f32[256,4,128]{2,0,1:T(8,128)S(1)}, ...), condition=%wide.wide.region_10.11_spmd.clone, body=%wide.wide.region_8.10_spmd.clone.sunk | while | flops 676028416 | bytes 12734739 | solution.py:100
  189.1 1.6 fusion.101
  192.1 1.6 convolution_add_fusion.7
  197.5 1.6 fusion.101
  200.4 1.6 convolution_add_fusion.7
  205.8 1.6 fusion.101
  208.8 1.6 convolution_add_fusion.7
  214.2 1.6 fusion.101
  217.1 1.6 convolution_add_fusion.7
  222.6 1.6 fusion.101
  225.5 1.6 convolution_add_fusion.7
  230.9 1.6 fusion.101
  233.9 1.6 convolution_add_fusion.7
  239.3 1.6 fusion.101
  242.3 1.6 convolution_add_fusion.7
  247.7 1.6 fusion.101
  250.6 1.6 convolution_add_fusion.7
  256.0 1.6 fusion.101
  259.0 1.6 convolution_add_fusion.7
  264.4 1.6 fusion.101
  267.4 1.6 convolution_add_fusion.7
  272.8 1.6 fusion.101
  275.7 1.6 convolution_add_fusion.7
  281.1 1.6 fusion.101
  284.1 1.6 convolution_add_fusion.7
  289.5 1.6 fusion.101
  292.5 1.6 convolution_add_fusion.7
  297.9 1.6 fusion.101
  300.8 1.6 convolution_add_fusion.7
  306.2 1.6 fusion.101
  309.2 1.6 convolution_add_fusion.7
  314.6 1.6 fusion.101
  317.5 1.6 convolution_add_fusion.7
  323.9 79.4 %reduce-scatter.5.cloned.1.call-done = f32[256,128]{1,0:T(8,128)} async-done(((f32[8192,128]{1,0:T(8,128)}), f32[256,128]{1,0:T(8,128)}) %reduce-scatter.5.cloned.1.call-update) | async-done | bytes 131088 | tf_op jit(solution)/shard_map/reduce_scatter | solution.py:158
  403.3 85.8 %reduce-scatter.3.cloned.1.call-done = f32[256,128]{1,0:T(8,128)} async-done(((f32[8192,128]{1,0:T(8,128)}), f32[256,128]{1,0:T(8,128)}) %reduce-scatter.3.cloned.1.call-update) | async-done | bytes 131088 | tf_op jit(solution)/shard_map/reduce_scatter | solution.py:157
  (298 shorter events, 136.0 us)
Async XLA Ops:
  7.2 3.1 copy-start
  7.2 13.5 %copy-start.3 = (s32[32,256]{1,0:T(8,128)S(1)}, s32[32,256]{1,0:T(8,128)}, u32[]{:S(2)}) copy-start(s32[32,256]{1,0:T(8,128)} %param.15) | copy-start | bytes 98308
  7.2 13.9 %copy-start.4 = (s32[16]{0:T(128)S(1)}, s32[16]{0:T(128)}, u32[]{:S(2)}) copy-start(s32[16]{0:T(128)} %param.14) | copy-start | bytes 196
  7.2 14.2 %copy-start.1 = (bf16[256,512]{1,0:T(8,128)(2,1)S(1)}, bf16[256,512]{1,0:T(8,128)(2,1)}, u32[]{:S(2)}) copy-start(bf16[256,512]{1,0:T(8,128)(2,1)} %param.13) | copy-start | bytes 786436
  7.2 49.5 %all-gather.3.cloned.1.call-start = ((), (), s32[]{:S(2)}) async-start(), calls=%async_computation.3 | async-start | bytes 2162688 | tf_op jit(solution)/shard_map/all_gather | solution.py:130
  7.9 94.0 %all-gather.5.cloned.1.call-start = ((), (), s32[]{:S(2)}) async-start(), calls=%async_computation.4 | async-start | bytes 2162688 | tf_op jit(solution)/shard_map/all_gather | solution.py:131
  12.2 17.5 %all-to-all-start = ((bf16[32,8,512]{2,1,0:T(8,128)(2,1)}), bf16[32,8,512]{2,1,0:T(8,128)(2,1)S(1)}, u32[]{:S(2)}, u32[]{:S(2)}) async-start(bf16[32,8,512]{2,1,0:T(8,128)(2,1)} %bitcast_select_fusion.2), calls=%async_computation | async-start | bytes 524288 | tf_op jit(solution)/shard_map/all_to_all | solution.py:115
  20.7 382.6 %reduce-scatter.5.cloned.1.call-start = ((), (), s32[]{:S(2)}) async-start(), calls=%async_computation.6 | async-start | bytes 4325376 | tf_op jit(solution)/shard_map/reduce_scatter | solution.py:158
  20.8 81.2 %copy-start.2 = (s32[32,8]{1,0:T(8,128)}, s32[32,8]{1,0:T(8,128)S(1)}, u32[]{:S(2)}) copy-start(s32[32,8]{1,0:T(8,128)S(1)} %dynamic-slice_add_fusion) | copy-start | bytes 3076
  321.4 167.7 %reduce-scatter.3.cloned.1.call-start = ((), (), s32[]{:S(2)}) async-start(), calls=%async_computation.5 | async-start | bytes 4325376 | tf_op jit(solution)/shard_map/reduce_scatter | solution.py:157
Sparse Core Ops, SparseCore 0:
  10.3 46.3 all-gather.2
  59.0 42.9 all-gather.4
  321.5 81.6 reduce-scatter.4
  407.3 81.6 reduce-scatter.2
where the time goes:
time: 498 us; the launch traced here: 496 us
  waiting for transfers between devices  247 us (50%)
  matrix products  160 us (32%)
  other arithmetic  41.9 us (8%)
  local copies, waits for them, and re-layouts  22.7 us (5%)
  between operations  14 us (3%)
  starting transfers between devices  8.6 us (2%)
    reduce_scatter x1, waiting for transfers between devices, per_device(): lax.psum_scatter(key_all, 'seq', scatter_dimension=0, tiled=True)  85.8 us
    reduce_scatter x1, waiting for transfers between devices, per_device(): lax.psum_scatter(value_all, 'seq', scatter_dimension=0, tiled=True)  79.4 us
    dot_general x32, matrix products, block_scores(): jnp.einsum('bhd,td->bht', query_heads, key_block, preferred_element_type=...  47.9 us
    all_gather x1, waiting for transfers between devices, per_device(): lax.all_gather(values, 'seq', axis=0, tiled=True)  45.3 us
    dot_general x16, matrix products, forward_update(): jnp.einsum('bht,td->bhd', exp_weights.astype(jnp.bfloat16), value_block,...  28.7 us
    all_gather x1, waiting for transfers between devices, per_device(): lax.all_gather(keys, 'seq', axis=0, tiled=True)  26.8 us
    dot_general x16, matrix products, backward_update(): jnp.einsum('bht,td->bhd', score_grads, key_block, preferred_element_type=...  24.8 us
    dot_general x16, matrix products, backward_update(): jnp.einsum('bhd,td->bht', grad_heads, value_block, preferred_element_type...  21.5 us
  transfers between devices with their start and end apart: 5, of which 5 were waited for; matrix products, arithmetic and copies ran while one was open for 1% of the time, Pallas kernels for 0%

commit v1 on v0

--- a/solution.py
+++ b/solution.py
@@ -5,6 +5,9 @@
 from jax.sharding import PartitionSpec as P
 
 masked_value = -1e30
+balance_cycles = lambda sample: jnp.concatenate(
+    lax.all_to_all(jnp.stack(lax.axis_size("seq") * [sample]), "seq", 0, 0), axis=0
+)
 
 
 def doc_index(positions, bounds):
@@ -126,10 +129,7 @@
         jnp.zeros((tok_rows, head_count), jnp.float32),
         jnp.zeros((tok_rows, head_count, head_dim), jnp.float32),
     )
-    piece_pair = (
-        lax.all_gather(keys, "seq", axis=0, tiled=True),
-        lax.all_gather(values, "seq", axis=0, tiled=True),
-    )
+    piece_pair = (lax.all_gather(keys, "seq", axis=0, tiled=True), balance_cycles(values))
     run_max, run_total, weighted = forward_piece(start_state, piece_pair[0], piece_pair[1], context)
     attended = weighted / run_total[:, :, None]
     attended_low = attended.astype(jnp.bfloat16)

time: 498 us -> 463 us (0.930)
  waiting for transfers between devices: 247 us -> 198 us
  blocking collectives: 0 us -> 17.2 us
    all_gather x1, waiting for transfers between devices: 45.3 us -> 0.02 us  [per_device(): lax.all_gather(values, 'seq', axis=0, tiled=True)]
    all_gather x1, waiting for transfers between devices: 26.8 us -> 2.88 us  [per_device(): lax.all_gather(keys, 'seq', axis=0, tiled=True)]
    all_to_all x1, waiting for transfers between devices: 7.96 us -> 28.7 us  [lax.all_to_all(jnp.stack(lax.axis_size('seq') * [sample]), 'seq', 0, 0)]
    all_to_all x0 -> x1, blocking collectives: none -> 17.2 us  [per_device(): lax.all_to_all(outgoing, 'seq', split_axis=0, concat_axis=0, tiled=True)]
  transfers between devices with their start and end apart: 5 -> 5, of which waited for: 5 -> 4; matrix products, arithmetic and copies ran while one was open for 1% -> 20% of each run, Pallas kernels for 0% -> 0%
where the time goes in v1:
time: 463 us; the launch traced here: 461 us
  waiting for transfers between devices  198 us (43%)
  matrix products  160 us (35%)
  other arithmetic  41.2 us (9%)
  local copies, waits for them, and re-layouts  24.5 us (5%)
  blocking collectives  17.2 us (4%)
  between operations  14 us (3%)
  starting transfers between devices  5.05 us (1%)
    reduce_scatter x1, waiting for transfers between devices, per_device(): lax.psum_scatter(key_all, 'seq', scatter_dimension=0, tiled=True)  85.8 us
    reduce_scatter x1, waiting for transfers between devices, per_device(): lax.psum_scatter(value_all, 'seq', scatter_dimension=0, tiled=True)  78.8 us
    dot_general x32, matrix products, block_scores(): jnp.einsum('bhd,td->bht', query_heads, key_block, preferred_element_type=...  47.9 us
    dot_general x16, matrix products, forward_update(): jnp.einsum('bht,td->bhd', exp_weights.astype(jnp.bfloat16), value_block,...  28.7 us
    all_to_all x1, waiting for transfers between devices, lax.all_to_all(jnp.stack(lax.axis_size('seq') * [sample]), 'seq', 0, 0)  28.7 us
    dot_general x16, matrix products, backward_update(): jnp.einsum('bht,td->bhd', score_grads, key_block, preferred_element_type=...  24.9 us
    dot_general x16, matrix products, backward_update(): jnp.einsum('bhd,td->bht', grad_heads, value_block, preferred_element_type...  21.5 us
    dynamic_slice x32, local copies, waits for them, and re-layouts, forward_piece(): run_state, _ = lax.scan(forward_update, run_state, stacked)  18.7 us
  transfers between devices with their start and end apart: 5, of which 4 were waited for; matrix products, arithmetic and copies ran while one was open for 20% of the time, Pallas kernels for 0%

profile of v1, /device:TPU:0, one launch (start us, length us, event | category | flops | bytes accessed | tf_op | source)
XLA Modules:
  0.0 461.3 jit_solution(13468308851842516548)
XLA Ops:
  10.7 17.2 %all_to_all.11 = bf16[32,8,512]{2,1,0:T(8,128)(2,1)S(1)} all-to-all(bf16[32,8,512]{2,1,0:T(8,128)(2,1)S(1)} %bitcast_select_fusion.2), channel_id=1, replica_groups=mesh['seq'=32,'head'=4] {'seq'}, dimensions={0} | all-to-all | bytes 524288 | tf_op jit(solution)/shard_map/all_to_all | solution.py:118
  27.9 1.8 stack.2
  29.7 4.9 %all-to-all-start.1 = ((bf16[32,256,128]{2,1,0:T(8,128)(2,1)}), bf16[32,256,128]{2,1,0:T(8,128)(2,1)}, u32[]{:S(2)}, u32[]{:S(2)}) async-start(bf16[32,256,128]{2,1,0:T(8,128)(2,1)} %stack.2), calls=%async_computation.1 | async-start | bytes 4194304 | tf_op jit(solution)/shard_map/all_to_all | solution.py:9
  36.6 28.7 %all-to-all-done.1 = bf16[32,256,128]{2,1,0:T(8,128)(2,1)} async-done(((bf16[32,256,128]{2,1,0:T(8,128)(2,1)}), bf16[32,256,128]{2,1,0:T(8,128)(2,1)}, u32[]{:S(2)}, u32[]{:S(2)}) %all-to-all-start.1) | async-done | bytes 2097184 | tf_op jit(solution)/shard_map/all_to_all | solution.py:9
  65.3 2.9 all-gather.3.cloned.1.call-done
  68.2 85.3 %while.32 = (s32[]{:T(128)}, f32[256,4]{0,1:T(4,128)S(1)}, f32[256,4]{0,1:T(4,128)S(1)}, f32[256,4,128]{2,0,1:T(8,128)S(1)}, s32[256]{0:T(256)S(1)}, /*index=5*/...) while((s32[]{:T(128)}, f32[256,4]{0,1:T(4,128)S(1)}, ...), condition=%wide.wide.region_6.7_spmd.clone, body=%wide.wide.region_2.6_spmd.clone.sunk | while | flops 276067328 | bytes 8466673 | solution.py:68
  69.8 1.4 fusion.88
  71.7 1.8 convolution_add_fusion.6
  75.1 1.4 fusion.88
  77.1 1.8 convolution_add_fusion.6
  80.4 1.4 fusion.88
  82.4 1.8 convolution_add_fusion.6
  87.7 1.8 convolution_add_fusion.6
  91.1 1.4 fusion.88
  93.0 1.8 convolution_add_fusion.6
  96.4 1.4 fusion.88
  98.4 1.8 convolution_add_fusion.6
  101.7 1.4 fusion.88
  103.7 1.8 convolution_add_fusion.6
  107.1 1.4 fusion.88
  109.1 1.8 convolution_add_fusion.6
  114.4 1.8 convolution_add_fusion.6
  119.7 1.8 convolution_add_fusion.6
  125.0 1.8 convolution_add_fusion.6
  130.4 1.8 convolution_add_fusion.6
  135.7 1.8 convolution_add_fusion.6
  141.0 1.8 convolution_add_fusion.6
  146.4 1.8 convolution_add_fusion.6
  151.7 1.8 convolution_add_fusion.6
  153.9 133.8 %while.33 = (s32[]{:T(128)}, f32[256,4,128]{2,0,1:T(8,128)S(1)}, f32[16,512,128]{2,1,0:T(8,128)}, f32[16,512,128]{2,1,0:T(8,128)}, s32[256]{0:T(256)S(1)}, /*ind...) while((s32[]{:T(128)}, f32[256,4,128]{2,0,1:T(8,128)S(1)}, ...), condition=%wide.wide.region_10.11_spmd.clone, body=%wide.wide.region_8.10_spmd.clone.sunk | while | flops 676028416 | bytes 12734739 | solution.py:103
  155.4 1.6 fusion.101
  158.4 1.6 convolution_add_fusion.7
  163.7 1.6 fusion.101
  166.7 1.6 convolution_add_fusion.7
  172.1 1.6 fusion.101
  175.0 1.6 convolution_add_fusion.7
  180.4 1.6 fusion.101
  183.4 1.6 convolution_add_fusion.7
  188.8 1.6 fusion.101
  191.8 1.6 convolution_add_fusion.7
  197.2 1.6 fusion.101
  200.2 1.6 convolution_add_fusion.7
  205.6 1.6 fusion.101
  208.5 1.6 convolution_add_fusion.7
  213.9 1.6 fusion.101
  216.9 1.6 convolution_add_fusion.7
  222.3 1.6 fusion.101
  225.3 1.6 convolution_add_fusion.7
  230.7 1.6 fusion.101
  233.6 1.6 convolution_add_fusion.7
  239.0 1.6 fusion.101
  242.0 1.6 convolution_add_fusion.7
  247.4 1.6 fusion.101
  250.4 1.6 convolution_add_fusion.7
  255.8 1.6 fusion.101
  258.7 1.6 convolution_add_fusion.7
  264.1 1.6 fusion.101
  267.1 1.6 convolution_add_fusion.7
  272.5 1.6 fusion.101
  275.4 1.6 convolution_add_fusion.7
  280.8 1.6 fusion.101
  283.8 1.6 convolution_add_fusion.7
  290.1 78.8 %reduce-scatter.5.cloned.1.call-done = f32[256,128]{1,0:T(8,128)} async-done(((f32[8192,128]{1,0:T(8,128)}), f32[256,128]{1,0:T(8,128)}) %reduce-scatter.5.cloned.1.call-update) | async-done | bytes 131088 | tf_op jit(solution)/shard_map/reduce_scatter | solution.py:158
  368.9 85.8 %reduce-scatter.3.cloned.1.call-done = f32[256,128]{1,0:T(8,128)} async-done(((f32[8192,128]{1,0:T(8,128)}), f32[256,128]{1,0:T(8,128)}) %reduce-scatter.3.cloned.1.call-update) | async-done | bytes 131088 | tf_op jit(solution)/shard_map/reduce_scatter | solution.py:157
  (302 shorter events, 136.7 us)
Async XLA Ops:
  7.2 2.3 copy-start
  7.2 20.7 %copy-start.1 = (bf16[256,128]{1,0:T(8,128)(2,1)S(1)}, bf16[256,128]{1,0:T(8,128)(2,1)}, u32[]{:S(2)}) copy-start(bf16[256,128]{1,0:T(8,128)(2,1)} %param.12) | copy-start | bytes 196612
  7.2 61.0 %all-gather.3.cloned.1.call-start = ((), (), s32[]{:S(2)}) async-start(), calls=%async_computation.4 | async-start | bytes 2162688 | tf_op jit(solution)/shard_map/all_gather | solution.py:132
  29.7 5.7 %copy-start.4 = (s32[32,256]{1,0:T(8,128)S(1)}, s32[32,256]{1,0:T(8,128)}, u32[]{:S(2)}) copy-start(s32[32,256]{1,0:T(8,128)} %param.15) | copy-start | bytes 98308
  29.7 6.1 %copy-start.5 = (s32[16]{0:T(128)S(1)}, s32[16]{0:T(128)}, u32[]{:S(2)}) copy-start(s32[16]{0:T(128)} %param.14) | copy-start | bytes 196
  29.7 6.4 %copy-start.2 = (bf16[256,512]{1,0:T(8,128)(2,1)S(1)}, bf16[256,512]{1,0:T(8,128)(2,1)}, u32[]{:S(2)}) copy-start(bf16[256,512]{1,0:T(8,128)(2,1)} %param.13) | copy-start | bytes 786436
  29.7 35.6 %all-to-all-start.1 = ((bf16[32,256,128]{2,1,0:T(8,128)(2,1)}), bf16[32,256,128]{2,1,0:T(8,128)(2,1)}, u32[]{:S(2)}, u32[]{:S(2)}) async-start(bf16[32,256,128]{2,1,0:T(8,128)(2,1)} %stack.2), calls=%async_computation.1 | async-start | bytes 4194304 | tf_op jit(solution)/shard_map/all_to_all | solution.py:9
  34.6 119.2 %all-gather.5.cloned.1.call-start = ((), (), s32[]{:S(2)}) async-start(), calls=%async_computation.5 | async-start | bytes 2162688 | tf_op jit(solution)/shard_map/all_gather | solution.py:150
  35.4 333.6 %reduce-scatter.5.cloned.1.call-start = ((), (), s32[]{:S(2)}) async-start(), calls=%async_computation.7 | async-start | bytes 4325376 | tf_op jit(solution)/shard_map/reduce_scatter | solution.py:158
  35.5 32.7 %copy-start.3 = (s32[32,8]{1,0:T(8,128)}, s32[32,8]{1,0:T(8,128)S(1)}, u32[]{:S(2)}) copy-start(s32[32,8]{1,0:T(8,128)S(1)} %dynamic-slice_add_fusion) | copy-start | bytes 3076
  287.7 167.1 %reduce-scatter.3.cloned.1.call-start = ((), (), s32[]{:S(2)}) async-start(), calls=%async_computation.6 | async-start | bytes 4325376 | tf_op jit(solution)/shard_map/reduce_scatter | solution.py:157
Sparse Core Ops, SparseCore 0:
  10.3 57.9 all-gather.2
  70.5 42.3 all-gather.4
  287.8 81.0 reduce-scatter.4
  373.0 81.7 reduce-scatter.2
